TPU v7x, 32 devices: a whole 2x2x4 slice. The times are simulated.
32 devices in a mesh: region: 2 (over y), tile: 4 (over z), corner: 2 (over x), kern: 2 (over core).
Axes of the slice: x: 2, y: 2, z: 4, core: 2. Of those that a mesh axis runs over, the one named last changes fastest.
Arguments:
- tile_mask: bfloat16 [16, 256, 256], P(('region', 'tile')), parts along dimension 0, may hold values from -1 to 1
- master_mask: bfloat16 [8, 256, 256], P(('region', 'tile')), parts along dimension 0, may hold values from -1 to 1
- target: bfloat16 [16, 256, 256], P(('region', 'tile')), parts along dimension 0, may hold values from 0 to 1
- inst_master: int32 [16], P(('region', 'tile')), parts along dimension 0, may hold values from 0 to 3, as said below
- inst_shift: int32 [16, 2], P(('region', 'tile')), parts along dimension 0, may hold values from 0 to 255
- kernels: float32 [2, 12, 2, 32, 32], P('corner'), may hold values from -24 to 24
- kernel_weight: float32 [2, 12], P('corner'), may hold values from 0.05 to 1
- corner_dose: float32 [2], P('corner'), may hold values from 0.6 to 1.6
Outputs:
- tile_grad: float32 [16, 256, 256], P(('region', 'tile')), parts along dimension 0
- master_grad: float32 [8, 256, 256], P(('region', 'tile')), parts along dimension 0
There are 2 independent parts, one for each index of `region`. A program takes and returns all parts, laid end to end along the dimension named above; an argument that names none is the same for every part. Nothing has to cross between parts.
Inputs may be any that keep to these rules, and one draw needn't show every extreme that they name: `inst_master`: each master cell is placed in exactly 2 tiles.
All inputs are finite; a program needn't handle non-finite values.
Results may differ from a plain program's by a relative error of at most 0.0003.
Values may be sent and summed in bfloat16 or wider, within the bound.
No kernel may reach another device: no remote copies, remote signals or barrier semaphores. Data moves between devices by JAX's collectives and lax.ppermute only.
A program may use at most 64 MiB of HBM per device.

v0:
```python
import math
import jax
import jax.numpy as jnp
from jax import lax
from jax.sharding import PartitionSpec as P

P_SIZE = 256
B = 32
precise = lax.Precision.HIGHEST
steepness = 3.0
threshold = 1.0


def band_tables():
    freq = jnp.arange(B, dtype=jnp.int32) - B // 2
    pixel = jnp.arange(P_SIZE, dtype=jnp.int32)
    angle = (
        2.0 * math.pi / P_SIZE * jnp.mod(freq[:, None] * pixel[None, :], P_SIZE).astype(jnp.float32)
    )
    return (jnp.cos(angle), -jnp.sin(angle))


def phase_ramp(shift):
    freq = jnp.arange(B, dtype=jnp.int32) - B // 2
    total = (
        freq[None, :, None] * shift[:, 0][:, None, None]
        + freq[None, None, :] * shift[:, 1][:, None, None]
    )
    angle = 2.0 * math.pi / P_SIZE * jnp.mod(total, P_SIZE).astype(jnp.float32)
    return (jnp.cos(angle), -jnp.sin(angle))


def spectra(masks, cos_tab, sin_tab):
    rows_re = jnp.einsum("bx,nxy->nby", cos_tab, masks, precision=precise)
    rows_im = jnp.einsum("bx,nxy->nby", sin_tab, masks, precision=precise)
    spec_re = jnp.einsum("nby,cy->nbc", rows_re, cos_tab, precision=precise) - jnp.einsum(
        "nby,cy->nbc", rows_im, sin_tab, precision=precise
    )
    spec_im = jnp.einsum("nby,cy->nbc", rows_re, sin_tab, precision=precise) + jnp.einsum(
        "nby,cy->nbc", rows_im, cos_tab, precision=precise
    )
    return (spec_re, spec_im)


def to_field(x_re, x_im, cos_tab, sin_tab, scale):
    half_re = jnp.einsum("bx,nbc->nxc", cos_tab, x_re, precision=precise) + jnp.einsum(
        "bx,nbc->nxc", sin_tab, x_im, precision=precise
    )
    half_im = jnp.einsum("bx,nbc->nxc", cos_tab, x_im, precision=precise) - jnp.einsum(
        "bx,nbc->nxc", sin_tab, x_re, precision=precise
    )
    out_re = (
        jnp.einsum("nxc,cy->nxy", half_re, cos_tab, precision=precise)
        + jnp.einsum("nxc,cy->nxy", half_im, sin_tab, precision=precise)
    ) * scale
    out_im = (
        jnp.einsum("nxc,cy->nxy", half_im, cos_tab, precision=precise)
        - jnp.einsum("nxc,cy->nxy", half_re, sin_tab, precision=precise)
    ) * scale
    return (out_re, out_im)


def back_pixels(x_re, x_im, cos_tab, sin_tab):
    half_re = jnp.einsum("bx,nbc->nxc", cos_tab, x_re, precision=precise) + jnp.einsum(
        "bx,nbc->nxc", sin_tab, x_im, precision=precise
    )
    half_im = jnp.einsum("bx,nbc->nxc", cos_tab, x_im, precision=precise) - jnp.einsum(
        "bx,nbc->nxc", sin_tab, x_re, precision=precise
    )
    return jnp.einsum("nxc,cy->nxy", half_re, cos_tab, precision=precise) + jnp.einsum(
        "nxc,cy->nxy", half_im, sin_tab, precision=precise
    )


def adjoint(g_re, g_im, cos_tab, sin_tab, scale):
    mid_re = jnp.einsum("bx,nxy->nby", cos_tab, g_re, precision=precise) - jnp.einsum(
        "bx,nxy->nby", sin_tab, g_im, precision=precise
    )
    mid_im = jnp.einsum("bx,nxy->nby", cos_tab, g_im, precision=precise) + jnp.einsum(
        "bx,nxy->nby", sin_tab, g_re, precision=precise
    )
    out_re = (
        jnp.einsum("nby,cy->nbc", mid_re, cos_tab, precision=precise)
        - jnp.einsum("nby,cy->nbc", mid_im, sin_tab, precision=precise)
    ) * scale
    out_im = (
        jnp.einsum("nby,cy->nbc", mid_re, sin_tab, precision=precise)
        + jnp.einsum("nby,cy->nbc", mid_im, cos_tab, precision=precise)
    ) * scale
    return (out_re, out_im)


def on_device(
    tile_mask, master_mask, target, inst_master, inst_shift, kernels, kernel_weight, corner_dose
):
    cos_tab, sin_tab = band_tables()
    scale = 1.0 / (P_SIZE * P_SIZE)
    local_tiles = tile_mask.shape[0]
    tile_re, tile_im = spectra(tile_mask.astype(jnp.float32), cos_tab, sin_tab)
    ph_re, ph_im = phase_ramp(inst_shift)

    def picker(count):
        index = jnp.arange(count, dtype=jnp.int32)
        return (inst_master[:, None] == index[None, :]).astype(jnp.float32)

    piece = lax.all_gather(master_mask, "tile", axis=0, tiled=True)
    chosen = picker(piece.shape[0])
    placed = jnp.einsum("tr,rxy->txy", chosen, piece.astype(jnp.float32), precision=precise)
    sel_re, sel_im = spectra(placed, cos_tab, sin_tab)
    spec_re = tile_re + (ph_re * sel_re - ph_im * sel_im)
    spec_im = tile_im + (ph_re * sel_im + ph_im * sel_re)
    goal = target.astype(jnp.float32)
    dose = corner_dose[0]
    kern_count = lax.axis_size("kern")
    kern_pos = lax.axis_index("kern")
    per_dev = kernels.shape[1] // kern_count
    first = kern_pos * per_dev
    mine_kern = lax.dynamic_slice_in_dim(kernels[0], first, per_dev, 0)
    kern_re = mine_kern[:, 0]
    kern_im = mine_kern[:, 1]
    weights = lax.dynamic_slice_in_dim(kernel_weight[0], first, per_dev, 0)

    def make_field(h_re, h_im):
        x_re = h_re * spec_re - h_im * spec_im
        x_im = h_re * spec_im + h_im * spec_re
        return to_field(x_re, x_im, cos_tab, sin_tab, scale)

    def forward(total, item):
        h_re, h_im, weight = item
        f_re, f_im = make_field(h_re, h_im)
        return (total + weight * (f_re * f_re + f_im * f_im), None)

    partial_light, unused = lax.scan(
        forward, jnp.zeros((local_tiles, P_SIZE, P_SIZE), jnp.float32), (kern_re, kern_im, weights)
    )
    intensity = lax.psum(partial_light, "kern")
    resist = jax.nn.sigmoid(steepness * (dose * intensity - threshold))
    sens = 2.0 * (resist - goal) * resist * (1.0 - resist) * steepness * dose

    def backward(acc, item):
        h_re, h_im, weight = item
        f_re, f_im = make_field(h_re, h_im)
        g_re = 2.0 * weight * sens * f_re
        g_im = 2.0 * weight * sens * f_im
        x_re, x_im = adjoint(g_re, g_im, cos_tab, sin_tab, scale)
        return ((acc[0] + h_re * x_re + h_im * x_im, acc[1] + h_re * x_im - h_im * x_re), None)

    zero = jnp.zeros((local_tiles, B, B), jnp.float32)
    grads, unused = lax.scan(backward, (zero, zero), (kern_re, kern_im, weights))
    partial_grad = jnp.stack([grads[0], grads[1]], axis=1)
    summed = lax.psum(partial_grad, ("corner", "kern"))
    tile_grad = back_pixels(summed[:, 0], summed[:, 1], cos_tab, sin_tab)
    back_re = ph_re * summed[:, 0] + ph_im * summed[:, 1]
    back_im = ph_re * summed[:, 1] - ph_im * summed[:, 0]
    masters_all = lax.axis_size("tile") * master_mask.shape[0]
    owner_pick = picker(masters_all)
    terms = jnp.stack(
        [
            jnp.einsum("tm,tbc->mbc", owner_pick, back_re, precision=precise),
            jnp.einsum("tm,tbc->mbc", owner_pick, back_im, precision=precise),
        ],
        axis=1,
    )
    mine = lax.psum_scatter(terms, "tile", scatter_dimension=0, tiled=True)
    master_grad = back_pixels(mine[:, 0], mine[:, 1], cos_tab, sin_tab)
    return (tile_grad, master_grad)


def solution(mesh):
    return jax.shard_map(
        on_device,
        mesh=mesh,
        in_specs=(
            P(("region", "tile"), None, None),
            P(("region", "tile"), None, None),
            P(("region", "tile"), None, None),
            P(("region", "tile")),
            P(("region", "tile"), None),
            P("corner", None, None, None, None),
            P("corner", None),
            P("corner"),
        ),
        out_specs=(P(("region", "tile"), None, None), P(("region", "tile"), None, None)),
        check_vma=False,
    )
```

profile of v0, /device:TPU:0, one launch (start us, length us, event | category | flops | bytes accessed | tf_op | source)
XLA Modules:
  0.0 199.7 jit_solution(11332372084410168777)
XLA Ops:
  7.2 17.7 %all_gather.3 = bf16[4,256,256]{2,1,0:T(8,128)(2,1)S(1)} all-gather(bf16[1,256,256]{2,1,0:T(8,128)(2,1)} %param.13), channel_id=1, replica_groups=mesh['region'=2,'tile'=4,'corner'=2,'kern'=2] {'tile'}, dimensions={0}, use_global_device_ids=true | all-gather | bytes 655360 | tf_op jit(solution)/shard_map/all_gather | solution.py:106
  32.3 37.9 %while.30 = (s32[]{:T(128)}, f32[2,256,256]{2,1,0:T(8,128)S(1)}, f32[6]{0:T(128)S(1)}, f32[6,32,32]{2,1,0:T(8,128)S(1)}, f32[2,32,32]{1,2,0:T(8,128)S(1)}, /*ind...) while((s32[]{:T(128)}, f32[2,256,256]{2,1,0:T(8,128)S(1)}, ...), condition=%wide.region_1.2_spmd.clone.clone.clone.clone, body=%wide.region_0.1_spmd.clone.clone.clone.clone.sunk | while | flops 228810752 | bytes 4981891 | solution.py:133
  37.0 1.6 fusion.466
  41.2 0.8 fusion.464
  43.3 1.6 fusion.466
  47.5 0.8 fusion.464
  49.7 1.6 fusion.466
  53.9 0.8 fusion.464
  56.0 1.6 fusion.466
  60.2 0.8 fusion.464
  62.3 1.6 fusion.466
  66.5 0.8 fusion.464
  68.6 1.6 fusion.466
  70.3 0.8 copy-done.1
  72.0 19.7 %all-reduce.2.cloned.1.call-done = f32[2,256,256]{2,1,0:T(8,128)} async-done(((f32[2,256,256]{2,1,0:T(8,128)}), f32[2,256,256]{2,1,0:T(8,128)}) %all-reduce.2.cloned.1.call-update) | async-done | bytes 524304 | tf_op jit(solution)/shard_map/psum | solution.py:136
  91.7 1.3 multiply_multiply_fusion
  93.0 61.6 %while.31 = (s32[]{:T(128)}, f32[2,32,32]{2,1,0:T(8,128)S(1)}, f32[2,32,32]{2,1,0:T(8,128)S(1)}, f32[6]{0:T(128)S(1)}, f32[2,256,256]{2,1,0:T(8,128)S(1)}, /*ind...) while((s32[]{:T(128)}, f32[2,32,32]{2,1,0:T(8,128)S(1)}, ...), condition=%wide.region_4.5_spmd.clone.clone.clone.clone, body=%wide.region_3.4_spmd.clone.clone.clone.clone.sunk | while | flops 456050688 | bytes 7833771 | solution.py:149
  96.8 0.8 fusion.502
  99.0 0.8 fusion.499
  107.1 0.8 fusion.502
  109.3 0.8 fusion.499
  119.5 0.8 fusion.499
  127.6 0.8 fusion.502
  129.8 0.8 fusion.499
  137.9 0.8 fusion.502
  140.1 0.8 fusion.499
  150.4 0.8 fusion.499
  154.7 12.2 %psum.15 = f32[2,2,32,32]{3,2,0,1:T(8,128)S(1)} all-reduce(f32[2,2,32,32]{3,2,0,1:T(8,128)S(1)} %pad_maximum_fusion.1), channel_id=1, replica_groups=mesh['region'=2,'tile'=4,'corner'=2,'kern'=2] {'corner','kern'}, use_global_device_ids=true, to_apply=%region_5.6 | all-reduce | flops 4096 | bytes 32768 | tf_op jit(solution)/shard_map/psum | solution.py:151
  170.9 1.6 convolution_add_fusion.6
  172.5 16.2 %reduce-scatter.2.cloned.1.call-done = f32[1,2,32,32]{3,2,1,0:T(8,128)} async-done(((f32[4,2,32,32]{3,2,1,0:T(8,128)}), f32[1,2,32,32]{3,2,1,0:T(8,128)}) %reduce-scatter.2.cloned.1.call-update) | async-done | bytes 8208 | tf_op jit(solution)/shard_map/reduce_scatter | solution.py:164
  188.7 1.1 fusion.250
  191.6 1.3 fusion.189
  (229 shorter events, 86.2 us)
Async XLA Ops:
  7.2 24.4 %copy-start = (f32[1,12,2,32,32]{4,3,2,1,0:T(8,128)S(1)}, f32[1,12,2,32,32]{4,3,2,1,0:T(8,128)}, u32[]{:S(2)}) copy-start(f32[1,12,2,32,32]{4,3,2,1,0:T(8,128)} %param.17) | copy-start | bytes 294916
  7.2 84.5 %all-reduce.2.cloned.1.call-start = ((), (), s32[]{:S(2)}) async-start(), calls=%async_computation.1 | async-start | bytes 1048576 | tf_op jit(solution)/shard_map/psum | solution.py:136
  7.2 17.7 %copy-start.4 = (s32[2]{0:T(128)S(1)}, s32[2]{0:T(128)}, u32[]{:S(2)}) copy-start(s32[2]{0:T(128)} %param.15) | copy-start | bytes 28
  26.7 1.0 copy-start.2
  29.7 0.7 copy-start.5
  31.6 0.7 copy-start.7
  70.3 0.8 copy-start.1
  70.3 21.4 %copy-start.3 = (bf16[2,256,256]{2,1,0:T(8,128)(2,1)S(1)}, bf16[2,256,256]{2,1,0:T(8,128)(2,1)}, u32[]{:S(2)}) copy-start(bf16[2,256,256]{2,1,0:T(8,128)(2,1)} %param.14) | copy-start | bytes 786436
  71.1 117.6 %reduce-scatter.2.cloned.1.call-start = ((), (), s32[]{:S(2)}) async-start(), calls=%async_computation.2 | async-start | bytes 163840 | tf_op jit(solution)/shard_map/reduce_scatter | solution.py:164
  188.7 1.2 copy-start.6
Sparse Core Ops, SparseCore 0:
  71.2 20.4 all-reduce.1
  169.5 19.2 reduce-scatter.1
where the time goes:
time: 200 us
  matrix products  99.7 us (50%)
  waiting for transfers between devices  36 us (18%)
  blocking collectives  29.9 us (15%)
  between operations  15 us (8%)
  local copies, waits for them, and re-layouts  11.7 us (6%)
  loops' own time  5.29 us (3%)
    psum x1, waiting for transfers between devices, on_device(): intensity = lax.psum(partial_light, 'kern')  19.7 us
    all_gather x1, blocking collectives, on_device(): piece = lax.all_gather(master_mask, 'tile', axis=0, tiled=True)  17.7 us
    reduce_scatter x1, waiting for transfers between devices, on_device(): mine = lax.psum_scatter(terms, 'tile', scatter_dimension=0, tiled=True)  16.2 us
    dot_general x12, matrix products, to_field(): jnp.einsum('nxc,cy->nxy', half_im, sin_tab, precision=precise)  14.3 us
    psum x1, blocking collectives, on_device(): summed = lax.psum(partial_grad, ('corner', 'kern'))  12.2 us
    dot_general x12, matrix products, to_field(): jnp.einsum('nxc,cy->nxy', half_re, sin_tab, precision=precise)  9.2 us
    dot_general x12, matrix products, to_field(): jnp.einsum('nxc,cy->nxy', half_im, cos_tab, precision=precise)  9.12 us
    dot_general x12, matrix products, to_field(): jnp.einsum('nxc,cy->nxy', half_re, cos_tab, precision=precise)  9.1 us
  transfers between devices with their start and end apart: 2, of which 2 were waited for; matrix products, arithmetic and copies ran while one was open for 2% of the time, Pallas kernels for 0%

commit v1 on v0

--- a/solution.py
+++ b/solution.py
@@ -133,7 +133,8 @@
     partial_light, unused = lax.scan(
         forward, jnp.zeros((local_tiles, P_SIZE, P_SIZE), jnp.float32), (kern_re, kern_im, weights)
     )
-    intensity = lax.psum(partial_light, "kern")
+    pieces = lax.all_gather(partial_light, "kern")
+    intensity = jnp.sum(pieces, axis=0)
     resist = jax.nn.sigmoid(steepness * (dose * intensity - threshold))
     sens = 2.0 * (resist - goal) * resist * (1.0 - resist) * steepness * dose
 

time: 200 us -> 191 us (0.955)
  waiting for transfers between devices: 36 us -> 26.3 us
    psum x1 -> x0, waiting for transfers between devices: 19.7 us -> none  [on_device(): intensity = lax.psum(partial_light, 'kern')]
    all_gather x0 -> x1, waiting for transfers between devices: none -> 10.1 us  [on_device(): pieces = lax.all_gather(partial_light, 'kern')]
where the time goes in v1:
time: 191 us; the launch traced here: 190 us
  matrix products  99.7 us (52%)
  blocking collectives  29.9 us (16%)
  waiting for transfers between devices  26.3 us (14%)
  between operations  15 us (8%)
  local copies, waits for them, and re-layouts  11.8 us (6%)
  loops' own time  5.29 us (3%)
  other arithmetic  2.06 us (1%)
    all_gather x1, blocking collectives, on_device(): piece = lax.all_gather(master_mask, 'tile', axis=0, tiled=True)  17.7 us
    reduce_scatter x1, waiting for transfers between devices, on_device(): mine = lax.psum_scatter(terms, 'tile', scatter_dimension=0, tiled=True)  16.2 us
    dot_general x12, matrix products, to_field(): jnp.einsum('nxc,cy->nxy', half_im, sin_tab, precision=precise)  14.3 us
    psum x1, blocking collectives, on_device(): summed = lax.psum(partial_grad, ('corner', 'kern'))  12.2 us
    all_gather x1, waiting for transfers between devices, on_device(): pieces = lax.all_gather(partial_light, 'kern')  10.1 us
    dot_general x12, matrix products, to_field(): jnp.einsum('nxc,cy->nxy', half_re, sin_tab, precision=precise)  9.22 us
    dot_general x12, matrix products, to_field(): jnp.einsum('nxc,cy->nxy', half_im, cos_tab, precision=precise)  9.12 us
    dot_general x12, matrix products, to_field(): jnp.einsum('nxc,cy->nxy', half_re, cos_tab, precision=precise)  9.1 us
  transfers between devices with their start and end apart: 2, of which 2 were waited for; matrix products, arithmetic and copies ran while one was open for 2% of the time, Pallas kernels for 0%

profile of v1, /device:TPU:0, one launch (start us, length us, event | category | flops | bytes accessed | tf_op | source)
XLA Modules:
  0.0 190.3 jit_solution(14073371318549059154)
XLA Ops:
  7.2 17.7 %all_gather.9 = bf16[4,256,256]{2,1,0:T(8,128)(2,1)S(1)} all-gather(bf16[1,256,256]{2,1,0:T(8,128)(2,1)} %param.13), channel_id=1, replica_groups=mesh['region'=2,'tile'=4,'corner'=2,'kern'=2] {'tile'}, dimensions={0}, use_global_device_ids=true | all-gather | bytes 655360 | tf_op jit(solution)/shard_map/all_gather | solution.py:106
  32.3 37.9 %while.30 = (s32[]{:T(128)}, f32[2,256,256]{2,1,0:T(8,128)S(1)}, f32[6]{0:T(128)S(1)}, f32[6,32,32]{2,1,0:T(8,128)S(1)}, f32[2,32,32]{1,2,0:T(8,128)S(1)}, /*ind...) while((s32[]{:T(128)}, f32[2,256,256]{2,1,0:T(8,128)S(1)}, ...), condition=%wide.region_1.2_spmd.clone.clone.clone.clone, body=%wide.region_0.1_spmd.clone.clone.clone.clone.sunk | while | flops 228810752 | bytes 4981891 | solution.py:133
  37.0 1.6 fusion.466
  41.2 0.8 fusion.464
  43.3 1.6 fusion.466
  47.5 0.8 fusion.464
  49.7 1.6 fusion.466
  56.0 1.6 fusion.466
  60.2 0.8 fusion.464
  62.3 1.6 fusion.466
  68.6 1.6 fusion.466
  70.3 0.8 copy-done.1
  72.0 10.1 %all-gather.3.cloned.1.call-done = f32[4,256,256]{2,1,0:T(8,128)} async-done(((f32[2,256,256]{2,1,0:T(8,128)}), f32[4,256,256]{2,1,0:T(8,128)}) %all-gather.3.cloned.1.call-update) | async-done | bytes 1048592 | tf_op jit(solution)/shard_map/all_gather | solution.py:136
  82.0 1.4 reduce_sum.9
  83.7 61.6 %while.31 = (s32[]{:T(128)}, f32[2,32,32]{2,1,0:T(8,128)S(1)}, f32[2,32,32]{2,1,0:T(8,128)S(1)}, f32[6]{0:T(128)S(1)}, f32[2,256,256]{2,1,0:T(8,128)S(1)}, /*ind...) while((s32[]{:T(128)}, f32[2,32,32]{2,1,0:T(8,128)S(1)}, ...), condition=%wide.region_4.5_spmd.clone.clone.clone.clone, body=%wide.region_3.4_spmd.clone.clone.clone.clone.sunk | while | flops 456050688 | bytes 7833771 | solution.py:150
  87.5 0.8 fusion.502
  89.7 0.8 fusion.499
  97.8 0.8 fusion.502
  99.9 0.8 fusion.499
  108.1 0.8 fusion.502
  110.2 0.8 fusion.499
  118.3 0.8 fusion.502
  120.5 0.8 fusion.499
  128.6 0.8 fusion.502
  130.8 0.8 fusion.499
  138.9 0.8 fusion.502
  141.0 0.8 fusion.499
  145.4 12.2 %psum.7 = f32[2,2,32,32]{3,2,0,1:T(8,128)S(1)} all-reduce(f32[2,2,32,32]{3,2,0,1:T(8,128)S(1)} %pad_maximum_fusion.1), channel_id=1, replica_groups=mesh['region'=2,'tile'=4,'corner'=2,'kern'=2] {'corner','kern'}, use_global_device_ids=true, to_apply=%region_5.6 | all-reduce | flops 4096 | bytes 32768 | tf_op jit(solution)/shard_map/psum | solution.py:152
  161.6 1.6 convolution_add_fusion.6
  163.2 16.2 %reduce-scatter.2.cloned.1.call-done = f32[1,2,32,32]{3,2,1,0:T(8,128)} async-done(((f32[4,2,32,32]{3,2,1,0:T(8,128)}), f32[1,2,32,32]{3,2,1,0:T(8,128)}) %reduce-scatter.2.cloned.1.call-update) | async-done | bytes 8208 | tf_op jit(solution)/shard_map/reduce_scatter | solution.py:165
  179.4 1.1 fusion.250
  182.2 1.3 fusion.189
  (230 shorter events, 86.4 us)
Async XLA Ops:
  7.2 24.4 %copy-start = (f32[1,12,2,32,32]{4,3,2,1,0:T(8,128)S(1)}, f32[1,12,2,32,32]{4,3,2,1,0:T(8,128)}, u32[]{:S(2)}) copy-start(f32[1,12,2,32,32]{4,3,2,1,0:T(8,128)} %param.17) | copy-start | bytes 294916
  7.2 74.9 %all-gather.3.cloned.1.call-start = ((), (), s32[]{:S(2)}) async-start(), calls=%async_computation.2 | async-start | bytes 1572864 | tf_op jit(solution)/shard_map/all_gather | solution.py:136
  7.2 17.7 %copy-start.4 = (s32[2]{0:T(128)S(1)}, s32[2]{0:T(128)}, u32[]{:S(2)}) copy-start(s32[2]{0:T(128)} %param.15) | copy-start | bytes 28
  26.7 1.0 copy-start.2
  29.7 0.7 copy-start.5
  31.6 0.7 copy-start.7
  70.3 0.8 copy-start.1
  71.1 108.3 %reduce-scatter.2.cloned.1.call-start = ((), (), s32[]{:S(2)}) async-start(), calls=%async_computation.1 | async-start | bytes 163840 | tf_op jit(solution)/shard_map/reduce_scatter | solution.py:165
  82.0 1.4 copy-start.3
  179.4 1.2 copy-start.6
Sparse Core Ops, SparseCore 0:
  71.2 10.7 all-gather.2
  160.1 19.2 reduce-scatter.1
